TPU v7x, 128 devices: a whole 4x4x4 slice. The times are simulated.
128 devices in a mesh: dom: 8 (over x, z_hi), grid: 16 (over z_lo, y, core).
Axes of the slice: x: 4, y: 4, z: 4 (z_hi: 2, z_lo: 2; z = z_hi * 2 + z_lo), core: 2. Of those that a mesh axis runs over, the one named last changes fastest.
Arguments:
- bands: float32 [8, 4, 64, 48, 1280], P('dom', None, None, 'grid'), may hold values from -6 to 6
- potential: float32 [4, 48, 32, 256], P(None, 'grid', 'dom'), may hold values from -1 to 1
- domain_blocks: int32 [8, 6], replicated, may hold values from 0 to 31, as said below
- block_slots: int32 [32], replicated, may hold values from 0 to 31, as said below
- domain_offsets: int32 [8], replicated, may hold values from 0 to 3
Outputs:
- filtered: float32 [8, 4, 64, 48, 1280], P('dom', None, None, 'grid')
Inputs may be any that keep to these rules, and one draw needn't show every extreme that they name: `domain_blocks`: each row is 6 cyclically consecutive logical blocks. `block_slots`: a permutation; slot // 4 is the index of dom that stores the block; no domain has more than 1 of its blocks stored on one index of dom, and some domain has exactly 1.
All inputs are finite; a program needn't handle non-finite values.
Results may differ from a plain program's by a relative error of at most 0.0003.
Values sent between devices are 32-bit elements; how exact they have to be, the bound alone decides.
No kernel may reach another device: no remote copies, remote signals or barrier semaphores. Data moves between devices by JAX's collectives and lax.ppermute only.
A program may use at most 128 MiB of HBM per device.

v0:
```python
import jax
import jax.numpy as jnp
from jax import lax
from jax.sharding import PartitionSpec as P

DZ = 64
OVL = 6
CELLS = 1280


e_half = 4.5
centre = 5.0
sigma_one = e_half / (-3.5 - centre)
sigma_two = 1.0 / (2.0 / sigma_one - sigma_one)
sigma_three = 1.0 / (2.0 / sigma_one - sigma_two)
rashba = 0.3


def extended(block, sides, width):
    for axis, dim in sides:
        count = lax.axis_size(axis)
        forward = [(i, i + 1) for i in range(count - 1)]
        backward = [(target, source) for source, target in forward]
        low = lax.ppermute(
            lax.slice_in_dim(block, block.shape[dim] - width, None, axis=dim), axis, forward
        )
        high = lax.ppermute(lax.slice_in_dim(block, 0, width, axis=dim), axis, backward)
        block = jnp.concatenate([low, block, high], axis=dim)
    return block


def along(field, steps):
    zeros = jnp.zeros(field.shape[:-1] + (abs(steps),), jnp.float32)
    if steps > 0:
        return jnp.concatenate([field[..., steps:], zeros], axis=-1)
    return jnp.concatenate([zeros, field[..., :steps]], axis=-1)


def apply_h(padded, fields):
    middle = padded[:, :, 1:-1]
    x_next = padded[:, :, 2:]
    x_prev = padded[:, :, :-2]
    cell_ids = jnp.arange(middle.shape[-1]) % DZ
    z_high = (cell_ids != DZ - 1).astype(jnp.float32)
    z_low = (cell_ids != 0).astype(jnp.float32)
    y_next = along(middle, DZ)
    y_prev = along(middle, -DZ)
    z_next = along(middle, 1) * z_high
    z_prev = along(middle, -1) * z_low
    lapl = x_next + x_prev + y_next + y_prev + z_next + z_prev - 6.0 * middle
    diff_x = 0.5 * (x_next - x_prev)
    diff_y = 0.5 * (y_next - y_prev)
    pot_v, mag_x, mag_y, mag_z = (
        fields[0][None],
        fields[1][None],
        fields[2][None],
        fields[3][None],
    )
    a_up, b_up, a_dn, b_dn = (middle[0], middle[1], middle[2], middle[3])
    out_a = (
        -0.5 * lapl[0]
        + pot_v * a_up
        + mag_z * a_up
        + mag_x * a_dn
        + mag_y * b_dn
        + rashba * (diff_y[3] + diff_x[2])
    )
    out_b = (
        -0.5 * lapl[1]
        + pot_v * b_up
        + mag_z * b_up
        + mag_x * b_dn
        - mag_y * a_dn
        + rashba * (diff_x[3] - diff_y[2])
    )
    out_c = (
        -0.5 * lapl[2]
        + pot_v * a_dn
        + mag_x * a_up
        - mag_y * b_up
        - mag_z * a_dn
        + rashba * (diff_y[1] - diff_x[0])
    )
    out_d = (
        -0.5 * lapl[3]
        + pot_v * b_dn
        + mag_x * b_up
        + mag_y * a_up
        - mag_z * b_dn
        - rashba * (diff_y[0] + diff_x[1])
    )
    return jnp.stack([out_a, out_b, out_c, out_d])


def neighbours(field):
    return extended(field, (("grid", 2),), 1)


def per_device(bands, potential, domain_blocks, block_slots, domain_offsets):
    spinors = bands[0]
    planes = spinors.shape[2]
    block_cells = potential.shape[3]
    domain = lax.axis_index("dom")
    slot_ids = block_slots[domain_blocks]
    gathered = lax.all_gather(potential, "dom", axis=2, tiled=True)
    picked = jnp.take(gathered, slot_ids[domain], axis=2)
    window = picked.reshape(4, planes, OVL * block_cells)
    first_cell = domain_offsets[domain] * DZ
    fields = lax.dynamic_slice_in_dim(window, first_cell, CELLS, 2)
    first = sigma_one / e_half * (apply_h(neighbours(spinors), fields) - centre * spinors)
    second = (
        2.0 * sigma_two / e_half * (apply_h(neighbours(first), fields) - centre * first)
        - sigma_one * sigma_two * spinors
    )
    third = (
        2.0 * sigma_three / e_half * (apply_h(neighbours(second), fields) - centre * second)
        - sigma_two * sigma_three * first
    )
    return third[None]


def solution(mesh):
    placed = (P("dom", None, None, "grid", None), P(None, "grid", "dom", None), P(), P(), P())
    return jax.shard_map(
        per_device,
        mesh=mesh,
        in_specs=placed,
        out_specs=P("dom", None, None, "grid", None),
        check_vma=False,
    )
```

profile of v0, /device:TPU:25, one launch (start us, length us, event | category | flops | bytes accessed | tf_op | source)
XLA Modules:
  0.0 171.0 jit_solution(2017998420111669350)
XLA Ops:
  0.0 2.0 %fusion.99 = (f32[4,64,1,1280]{3,1,2,0:T(8,128)S(1)}, f32[4,64,1,1280]{3,1,2,0:T(8,128)S(1)}) fusion(f32[4,64,3,1280]{3,1,2,0:T(8,128)} %bitcast.95), kind=kLoop, calls=%fused_computation.176 | loop fusion | bytes 5242880 | tf_op jit(solution)/shard_map/slice | solution.py:25
  2.0 3.8 %collective-permute-start.1 = (f32[4,64,1,1280]{3,1,2,0:T(8,128)S(1)}, f32[4,64,1,1280]{3,1,2,0:T(8,128)}, u32[]{:S(2)}, u32[]{:S(2)}) collective-permute-start(f32[4,64,1,1280]{3,1,2,0:T(8,128)S(1)} %get-tuple-element.41), channel_id=1, source_target_pairs={{0,1},{1,2},{2,3},{3,4},{4,5},{5,6},{6,7},{7,8},{8,9},{9,10},{10,1... | collective-permute-start | bytes 3932168 | tf_op jit(solution)/shard_map/ppermute | solution.py:24
  8.8 7.6 %fusion.97 = (f32[4,64,3,1279]{3,1,2,0:T(8,128)}, f32[4,64,3,1279]{3,1,2,0:T(8,128)}) fusion(f32[4,64,3,1280]{3,1,2,0:T(8,128)} %bitcast.96), kind=kLoop, calls=%fused_computation.174 | loop fusion | bytes 15716352 | tf_op jit(solution)/shard_map/slice | solution.py:35
  17.8 28.8 %all_gather.3 = f32[4,3,32,256]{3,0,2,1:T(4,128)S(1)} all-gather(f32[4,3,4,256]{3,0,2,1:T(4,128)S(1)} %copy.6), channel_id=1, replica_groups=mesh['dom'=8,'grid'=16] {'dom'}, dimensions={2}, use_global_device_ids=true | all-gather | bytes 442368 | tf_op jit(solution)/shard_map/all_gather | solution.py:105
  47.5 7.7 %fusion.98 = (f32[4,64,3,1216]{3,1,2,0:T(8,128)}, f32[4,64,3,1216]{3,1,2,0:T(8,128)}) fusion(f32[4,64,3,1280]{3,1,2,0:T(8,128)} %bitcast.97), kind=kLoop, calls=%fused_computation.175 | loop fusion | bytes 14942208 | tf_op jit(solution)/shard_map/slice | solution.py:35
  55.3 8.5 %multiply_subtract_fusion.2 = (f32[4,64,3,1280]{3,1,2,0:T(8,128)S(1)}, f32[4,64,3,1280]{3,1,2,0:T(8,128)}, f32[4,64,3,1280]{3,1,2,0:T(8,128)}) fusion(f32[4,64,3,1280]{3,1,2,0:T(8,128)S(1)} %bitcast.98, f32[4,64,3,1279]{3,1,2,0:T(8,128)} %get-tuple-element.38, f32[4,64,3,1279]{3,1,2,0:T(8,128)S(1)} %copy-done.11, f32[4,64,3,1216]{3,1,2,0:T(8,128)} %get-tuple-element.40, ...), kind=kLoop, calls=%fused_computation.28 | loop fusion | flops 14745600 | bytes 33689600 | tf_op jit(solution)/shard_map/sub | solution.py:50
  63.8 3.5 %fusion.72 = (f32[1,64,3,1280]{3,1,2,0:T(8,128)S(1)}, f32[1,64,3,1280]{3,1,2,0:T(8,128)S(1)}) fusion(f32[4,64,3,1280]{3,1,2,0:T(8,128)} %get-tuple-element.22, f32[4,64,3,1280]{3,1,2,0:T(8,128)} %get-tuple-element.24, f32[4,64,3,1280]{3,1,2,0:T(8,128)S(1)} %get-tuple-element.21, f32[1,4,64,3,1280]{4,2,3,1,0:T(8,128)S(1)} %copy-done.2, ...), kind=kLoop, calls=%fused_computation.116 | loop fusion | flops 5898240 | bytes 11857920 | tf_op jit(solution)/shard_map/add | solution.py:69
  70.1 11.8 %collective-permute-start.3 = (f32[4,64,1,1280]{3,1,2,0:T(8,128)S(1)}, f32[4,64,1,1280]{3,1,2,0:T(8,128)S(1)}, u32[]{:S(2)}, u32[]{:S(2)}) collective-permute-start(f32[4,64,1,1280]{3,1,2,0:T(8,128)S(1)} %get-tuple-element.35), channel_id=1, source_target_pairs={{0,1},{1,2},{2,3},{3,4},{4,5},{5,6},{6,7},{7,8},{8,9},{9,10},{10,1... | collective-permute-start | bytes 3932168 | tf_op jit(solution)/shard_map/ppermute | solution.py:24
  82.0 2.1 %collective-permute-start.2 = (f32[4,64,1,1280]{3,1,2,0:T(8,128)S(1)}, f32[4,64,1,1280]{3,1,2,0:T(8,128)S(1)}, u32[]{:S(2)}, u32[]{:S(2)}) collective-permute-start(f32[4,64,1,1280]{3,1,2,0:T(8,128)S(1)} %get-tuple-element.36), channel_id=1, source_target_pairs={{1,0},{2,1},{3,2},{4,3},{5,4},{6,5},{7,6},{8,7},{9,8},{10,9},{11,1... | collective-permute-start | bytes 3932168 | tf_op jit(solution)/shard_map/ppermute | solution.py:27
  84.1 4.4 %fusion.94 = (f32[4,64,3,1279]{3,1,2,0:T(8,128)}, f32[4,64,3,1279]{3,1,2,0:T(8,128)}) fusion(f32[4,64,3,1280]{3,1,2,0:T(8,128)S(1)} %broadcast_multiply_fusion), kind=kLoop, calls=%fused_computation.171 | loop fusion | bytes 15716352 | tf_op jit(solution)/shard_map/slice | solution.py:35
  88.5 4.4 %fusion.95 = (f32[4,64,3,1216]{3,1,2,0:T(8,128)}, f32[4,64,3,1216]{3,1,2,0:T(8,128)}) fusion(f32[4,64,3,1280]{3,1,2,0:T(8,128)S(1)} %broadcast_multiply_fusion), kind=kLoop, calls=%fused_computation.172 | loop fusion | bytes 14942208 | tf_op jit(solution)/shard_map/slice | solution.py:35
  93.0 3.6 %collective-permute-done.3 = f32[4,64,1,1280]{3,1,2,0:T(8,128)S(1)} collective-permute-done((f32[4,64,1,1280]{3,1,2,0:T(8,128)S(1)}, f32[4,64,1,1280]{3,1,2,0:T(8,128)S(1)}, u32[]{:S(2)}, u32[]{:S(2)}) %collective-permute-start.3) | collective-permute-done | bytes 1310752 | tf_op jit(solution)/shard_map/ppermute | solution.py:24
  96.5 6.5 %collective-permute-done.2 = f32[4,64,1,1280]{3,1,2,0:T(8,128)S(1)} collective-permute-done((f32[4,64,1,1280]{3,1,2,0:T(8,128)S(1)}, f32[4,64,1,1280]{3,1,2,0:T(8,128)S(1)}, u32[]{:S(2)}, u32[]{:S(2)}) %collective-permute-start.2) | collective-permute-done | bytes 1310752 | tf_op jit(solution)/shard_map/ppermute | solution.py:27
  103.0 2.5 %subtract_multiply_fusion.2 = f32[4,64,3,1280]{3,1,2,0:T(8,128)} fusion(f32[4,64,1,1280]{3,1,2,0:T(8,128)S(1)} %collective-permute-done.2, f32[4,64,3,1280]{3,1,2,0:T(8,128)S(1)} %broadcast_multiply_fusion, f32[4,64,1,1280]{3,1,2,0:T(8,128)S(1)} %collective-permute-done.3), kind=kLoop, calls=%fused_computation.23 | loop fusion | flops 3932160 | bytes 10485760 | tf_op jit(solution)/shard_map/mul | solution.py:51
  105.5 9.3 %multiply_subtract_fusion.1 = (f32[4,64,3,1280]{3,1,2,0:T(8,128)}, f32[4,64,3,1280]{3,1,2,0:T(8,128)}) fusion(f32[4,64,3,1279]{3,1,2,0:T(8,128)} %get-tuple-element.32, f32[4,64,3,1279]{3,1,2,0:T(8,128)} %get-tuple-element.31, f32[4,64,3,1216]{3,1,2,0:T(8,128)} %get-tuple-element.34, f32[4,64,3,1216]{3,1,2,0:T(8,128)} %get-tuple-element.33, ...), kind=kLoop, calls=%fused_computation.25 | loop fusion | flops 17694720 | bytes 37621760 | tf_op jit(solution)/shard_map/sub | solution.py:50
  114.8 4.1 %fusion.48 = (f32[1,64,3,1280]{3,1,2,0:T(8,128)S(1)}, f32[1,64,3,1280]{3,1,2,0:T(8,128)S(1)}) fusion(f32[4,64,3,1280]{3,1,2,0:T(8,128)} %get-tuple-element.20, f32[4,64,3,1280]{3,1,2,0:T(8,128)} %subtract_multiply_fusion.2, f32[4,64,3,1280]{3,1,2,0:T(8,128)} %get-tuple-element.19, f32[4,64,3,1280]{3,1,2,0:T(8,128)S(1)} %broadcast_multiply_fusion, ...), kind=kLoop, calls=%fused_computation.84 | loop fusion | flops 5898240 | bytes 11857920 | tf_op jit(solution)/shard_map/add | solution.py:69
  125.4 2.6 %collective-permute-start.4 = (f32[4,64,1,1280]{3,1,2,0:T(8,128)S(1)}, f32[4,64,1,1280]{3,1,2,0:T(8,128)S(1)}, u32[]{:S(2)}, u32[]{:S(2)}) collective-permute-start(f32[4,64,1,1280]{3,1,2,0:T(8,128)S(1)} %get-tuple-element.30), channel_id=1, source_target_pairs={{1,0},{2,1},{3,2},{4,3},{5,4},{6,5},{7,6},{8,7},{9,8},{10,9},{11,1... | collective-permute-start | bytes 3932168 | tf_op jit(solution)/shard_map/ppermute | solution.py:27
  128.0 4.5 %fusion.92 = (f32[4,64,3,1216]{3,1,2,0:T(8,128)}, f32[4,64,3,1216]{3,1,2,0:T(8,128)}) fusion(f32[4,64,3,1280]{3,1,2,0:T(8,128)S(1)} %fusion.1), kind=kLoop, calls=%fused_computation.169 | loop fusion | bytes 14942208 | tf_op jit(solution)/shard_map/slice | solution.py:35
  132.5 4.5 %fusion.91 = (f32[4,64,3,1279]{3,1,2,0:T(8,128)}, f32[4,64,3,1279]{3,1,2,0:T(8,128)}) fusion(f32[4,64,3,1280]{3,1,2,0:T(8,128)S(1)} %fusion.1), kind=kLoop, calls=%fused_computation.168 | loop fusion | bytes 15716352 | tf_op jit(solution)/shard_map/slice | solution.py:35
  137.1 2.9 %collective-permute-done.5 = f32[4,64,1,1280]{3,1,2,0:T(8,128)S(1)} collective-permute-done((f32[4,64,1,1280]{3,1,2,0:T(8,128)S(1)}, f32[4,64,1,1280]{3,1,2,0:T(8,128)S(1)}, u32[]{:S(2)}, u32[]{:S(2)}) %collective-permute-start.5) | collective-permute-done | bytes 1310752 | tf_op jit(solution)/shard_map/ppermute | solution.py:24
  139.9 6.5 %collective-permute-done.4 = f32[4,64,1,1280]{3,1,2,0:T(8,128)S(1)} collective-permute-done((f32[4,64,1,1280]{3,1,2,0:T(8,128)S(1)}, f32[4,64,1,1280]{3,1,2,0:T(8,128)S(1)}, u32[]{:S(2)}, u32[]{:S(2)}) %collective-permute-start.4) | collective-permute-done | bytes 1310752 | tf_op jit(solution)/shard_map/ppermute | solution.py:27
  147.6 10.7 %multiply_subtract_fusion = (f32[4,64,3,1280]{3,1,2,0:T(8,128)}, f32[4,64,3,1280]{3,1,2,0:T(8,128)}, f32[4,64,3,1280]{3,1,2,0:T(8,128)}) fusion(f32[4,64,3,1280]{3,1,2,0:T(8,128)S(1)} %fusion.1, f32[4,64,3,1279]{3,1,2,0:T(8,128)} %get-tuple-element.26, f32[4,64,3,1279]{3,1,2,0:T(8,128)} %get-tuple-element.25, f32[4,64,3,1216]{3,1,2,0:T(8,128)} %get-tuple-element.28, ...), kind=kLoop, calls=%fused_computation.22 | loop fusion | flops 14745600 | bytes 33689600 | tf_op jit(solution)/shard_map/sub | solution.py:50
  158.4 4.1 %fusion.23 = (f32[1,1,64,3,1280]{4,2,3,1,0:T(8,128)S(1)}, f32[1,1,64,3,1280]{4,2,3,1,0:T(8,128)S(1)}) fusion(f32[4,64,3,1280]{3,1,2,0:T(8,128)} %get-tuple-element.18, f32[4,64,3,1280]{3,1,2,0:T(8,128)} %get-tuple-element.23, f32[4,64,3,1280]{3,1,2,0:T(8,128)} %get-tuple-element.17, f32[4,64,3,1280]{3,1,2,0:T(8,128)S(1)} %fusion.1, ...), kind=kLoop, calls=%fused_computation.51 | loop fusion | flops 5898240 | bytes 11857920 | tf_op jit(solution)/shard_map/stack | solution.py:92
  166.5 4.5 %fusion.3 = f32[1,4,64,3,1280]{4,2,3,1,0:T(8,128)} fusion(f32[1,1,64,3,1280]{4,2,3,1,0:T(8,128)} %get-tuple-element.6, f32[1,1,64,3,1280]{4,2,3,1,0:T(8,128)S(1)} %get-tuple-element.8, f32[1,1,64,3,1280]{4,2,3,1,0:T(8,128)S(1)} %get-tuple-element.7, f32[1,1,64,3,1280]{4,2,3,1,0:T(8,128)S(1)} %get-tuple-element.5, f32[1,1,64,3,1280]{4,2,3,1,0:T(8,128)S(1)} %bitcast.106, ...), kind=kLoop, calls=%fused_computation.14 | loop fusion | flops 20643840 | bytes 19660800 | tf_op jit(solution)/shard_map/sub | solution.py:116
  (73 shorter events, 19.1 us)
Async XLA Ops:
  0.0 7.8 %copy-start = (s32[32]{0:T(128)S(1)}, s32[32]{0:T(128)}, u32[]{:S(2)}) copy-start(s32[32]{0:T(128)} %param.8) | copy-start | bytes 388
  0.0 7.7 %copy-start.19 = (s32[8,6]{1,0:T(8,128)S(1)}, s32[8,6]{1,0:T(8,128)}, u32[]{:S(2)}) copy-start(s32[8,6]{1,0:T(8,128)} %param.7) | copy-start | bytes 580
  2.0 53.3 %collective-permute-start.1 = (f32[4,64,1,1280]{3,1,2,0:T(8,128)S(1)}, f32[4,64,1,1280]{3,1,2,0:T(8,128)}, u32[]{:S(2)}, u32[]{:S(2)}) collective-permute-start(f32[4,64,1,1280]{3,1,2,0:T(8,128)S(1)} %get-tuple-element.41), channel_id=1, source_target_pairs={{0,1},{1,2},{2,3},{3,4},{4,5},{5,6},{6,7},{7,8},{8,9},{9,10},{10,1... | collective-permute-start | bytes 3932168 | tf_op jit(solution)/shard_map/ppermute | solution.py:24
  5.8 49.5 %collective-permute-start = (f32[4,64,1,1280]{3,1,2,0:T(8,128)S(1)}, f32[4,64,1,1280]{3,1,2,0:T(8,128)}, u32[]{:S(2)}, u32[]{:S(2)}) collective-permute-start(f32[4,64,1,1280]{3,1,2,0:T(8,128)S(1)} %get-tuple-element.42), channel_id=1, source_target_pairs={{1,0},{2,1},{3,2},{4,3},{5,4},{6,5},{7,6},{8,7},{9,8},{10,9},{11,1... | collective-permute-start | bytes 3932168 | tf_op jit(solution)/shard_map/ppermute | solution.py:27
  8.7 7.7 %copy-start.20 = (s32[8]{0:T(128)S(1)}, s32[8]{0:T(128)}, u32[]{:S(2)}) copy-start(s32[8]{0:T(128)} %param.9) | copy-start | bytes 100
  8.7 9.0 %copy-start.18 = (f32[4,3,4,256]{3,2,1,0:T(4,128)S(1)}, f32[4,3,4,256]{3,2,1,0:T(4,128)}, u32[]{:S(2)}) copy-start(f32[4,3,4,256]{3,2,1,0:T(4,128)} %param.6) | copy-start | bytes 147460
  47.5 7.8 %copy-start.2 = (f32[1,4,64,3,1280]{4,2,3,1,0:T(8,128)S(1)}, f32[1,4,64,3,1280]{4,2,3,1,0:T(8,128)}, u32[]{:S(2)}) copy-start(f32[1,4,64,3,1280]{4,2,3,1,0:T(8,128)} %param.5) | copy-start | bytes 11796484
  47.5 7.8 %copy-start.11 = (f32[4,64,3,1279]{3,1,2,0:T(8,128)S(1)}, f32[4,64,3,1279]{3,1,2,0:T(8,128)}, u32[]{:S(2)}) copy-start(f32[4,64,3,1279]{3,1,2,0:T(8,128)} %get-tuple-element.37) | copy-start | bytes 11787268
  63.8 3.5 %copy-start.9 = (f32[4,64,3,1280]{3,1,2,0:T(8,128)S(1)}, f32[4,64,3,1280]{3,1,2,0:T(8,128)}, u32[]{:S(2)}) copy-start(f32[4,64,3,1280]{3,1,2,0:T(8,128)} %get-tuple-element.22) | copy-start | bytes 11796484
  63.8 4.5 %copy-start.10 = (f32[4,64,3,1280]{3,1,2,0:T(8,128)S(1)}, f32[4,64,3,1280]{3,1,2,0:T(8,128)}, u32[]{:S(2)}) copy-start(f32[4,64,3,1280]{3,1,2,0:T(8,128)} %get-tuple-element.24) | copy-start | bytes 11796484
  70.1 26.4 %collective-permute-start.3 = (f32[4,64,1,1280]{3,1,2,0:T(8,128)S(1)}, f32[4,64,1,1280]{3,1,2,0:T(8,128)S(1)}, u32[]{:S(2)}, u32[]{:S(2)}) collective-permute-start(f32[4,64,1,1280]{3,1,2,0:T(8,128)S(1)} %get-tuple-element.35), channel_id=1, source_target_pairs={{0,1},{1,2},{2,3},{3,4},{4,5},{5,6},{6,7},{7,8},{8,9},{9,10},{10,1... | collective-permute-start | bytes 3932168 | tf_op jit(solution)/shard_map/ppermute | solution.py:24
  82.0 21.0 %collective-permute-start.2 = (f32[4,64,1,1280]{3,1,2,0:T(8,128)S(1)}, f32[4,64,1,1280]{3,1,2,0:T(8,128)S(1)}, u32[]{:S(2)}, u32[]{:S(2)}) collective-permute-start(f32[4,64,1,1280]{3,1,2,0:T(8,128)S(1)} %get-tuple-element.36), channel_id=1, source_target_pairs={{1,0},{2,1},{3,2},{4,3},{5,4},{6,5},{7,6},{8,7},{9,8},{10,9},{11,1... | collective-permute-start | bytes 3932168 | tf_op jit(solution)/shard_map/ppermute | solution.py:27
  114.8 4.1 %copy-start.3 = (f32[4,64,3,1280]{3,1,2,0:T(8,128)S(1)}, f32[4,64,3,1280]{3,1,2,0:T(8,128)}, u32[]{:S(2)}) copy-start(f32[4,64,3,1280]{3,1,2,0:T(8,128)} %subtract_multiply_fusion.2) | copy-start | bytes 11796484
  114.8 5.1 %copy-start.4 = (f32[4,64,3,1280]{3,1,2,0:T(8,128)S(1)}, f32[4,64,3,1280]{3,1,2,0:T(8,128)}, u32[]{:S(2)}) copy-start(f32[4,64,3,1280]{3,1,2,0:T(8,128)} %get-tuple-element.19) | copy-start | bytes 11796484
  114.8 6.2 %copy-start.5 = (f32[4,64,3,1280]{3,1,2,0:T(8,128)S(1)}, f32[4,64,3,1280]{3,1,2,0:T(8,128)}, u32[]{:S(2)}) copy-start(f32[4,64,3,1280]{3,1,2,0:T(8,128)} %get-tuple-element.20) | copy-start | bytes 11796484
  123.5 16.5 %collective-permute-start.5 = (f32[4,64,1,1280]{3,1,2,0:T(8,128)S(1)}, f32[4,64,1,1280]{3,1,2,0:T(8,128)S(1)}, u32[]{:S(2)}, u32[]{:S(2)}) collective-permute-start(f32[4,64,1,1280]{3,1,2,0:T(8,128)S(1)} %get-tuple-element.29), channel_id=1, source_target_pairs={{0,1},{1,2},{2,3},{3,4},{4,5},{5,6},{6,7},{7,8},{8,9},{9,10},{10,1... | collective-permute-start | bytes 3932168 | tf_op jit(solution)/shard_map/ppermute | solution.py:24
  125.4 21.0 %collective-permute-start.4 = (f32[4,64,1,1280]{3,1,2,0:T(8,128)S(1)}, f32[4,64,1,1280]{3,1,2,0:T(8,128)S(1)}, u32[]{:S(2)}, u32[]{:S(2)}) collective-permute-start(f32[4,64,1,1280]{3,1,2,0:T(8,128)S(1)} %get-tuple-element.30), channel_id=1, source_target_pairs={{1,0},{2,1},{3,2},{4,3},{5,4},{6,5},{7,6},{8,7},{9,8},{10,9},{11,1... | collective-permute-start | bytes 3932168 | tf_op jit(solution)/shard_map/ppermute | solution.py:27
  139.9 6.5 %copy-start.16 = (f32[4,64,1,1280]{3,1,2,0:T(8,128)}, f32[4,64,1,1280]{3,1,2,0:T(8,128)S(1)}, u32[]{:S(2)}) copy-start(f32[4,64,1,1280]{3,1,2,0:T(8,128)S(1)} %collective-permute-done.5) | copy-start | bytes 3932164
  158.3 4.1 %copy-start.6 = (f32[4,64,3,1280]{3,1,2,0:T(8,128)S(1)}, f32[4,64,3,1280]{3,1,2,0:T(8,128)}, u32[]{:S(2)}) copy-start(f32[4,64,3,1280]{3,1,2,0:T(8,128)} %get-tuple-element.17) | copy-start | bytes 11796484
  158.3 5.1 %copy-start.7 = (f32[4,64,3,1280]{3,1,2,0:T(8,128)S(1)}, f32[4,64,3,1280]{3,1,2,0:T(8,128)}, u32[]{:S(2)}) copy-start(f32[4,64,3,1280]{3,1,2,0:T(8,128)} %get-tuple-element.18) | copy-start | bytes 11796484
  158.3 6.2 %copy-start.8 = (f32[4,64,3,1280]{3,1,2,0:T(8,128)S(1)}, f32[4,64,3,1280]{3,1,2,0:T(8,128)}, u32[]{:S(2)}) copy-start(f32[4,64,3,1280]{3,1,2,0:T(8,128)} %get-tuple-element.23) | copy-start | bytes 11796484
  164.5 2.0 %copy-start.13 = (f32[1,64,3,1280]{3,1,2,0:T(8,128)S(1)}, f32[1,64,3,1280]{3,1,2,0:T(8,128)}, u32[]{:S(2)}) copy-start(f32[1,64,3,1280]{3,1,2,0:T(8,128)} %copy-done.12) | copy-start | bytes 2949124
  164.5 2.0 %copy-start.15 = (f32[1,64,3,1280]{3,1,2,0:T(8,128)S(1)}, f32[1,64,3,1280]{3,1,2,0:T(8,128)}, u32[]{:S(2)}) copy-start(f32[1,64,3,1280]{3,1,2,0:T(8,128)} %copy-done.14) | copy-start | bytes 2949124
  166.5 4.5 %copy-start.1 = (s32[32]{0:T(128)S(1)}, s32[32]{0:T(128)}, u32[]{:S(2)}) copy-start(s32[32]{0:T(128)} %param.8) | copy-start | bytes 388
  (3 other events, 3.6 us)
where the time goes:
time: 171 us
  other arithmetic  53 us (31%)
  local copies, waits for them, and re-layouts  44.6 us (26%)
  blocking collectives  28.8 us (17%)
  starting transfers between devices  24.2 us (14%)
  waiting for transfers between devices  19.4 us (11%)
    slice x6, local copies, waits for them, and re-layouts, along(): return jnp.concatenate([field[..., steps:], zeros], axis=-1)  33.3 us
    all_gather x1, blocking collectives, per_device(): gathered = lax.all_gather(potential, 'dom', axis=2, tiled=True)  28.8 us
    sub x3, other arithmetic, apply_h(): lapl = x_next + x_prev + y_next + y_prev + z_next + z_prev - 6.0 * middle  28.5 us
    ppermute x3, starting transfers between devices, extended(): lax.ppermute(lax.slice_in_dim(block, block.shape[dim] - width, None, axis...  17.5 us
    ppermute x3, waiting for transfers between devices, extended(): lax.ppermute(lax.slice_in_dim(block, 0, width, axis=dim), axis, backward)  13 us
    add x2, other arithmetic, apply_h(): -0.5 * lapl[1] + pot_v * b_up + mag_z * b_up + mag_x * b_dn - mag_y * a_dn  7.52 us
    ppermute x3, starting transfers between devices, extended(): lax.ppermute(lax.slice_in_dim(block, 0, width, axis=dim), axis, backward)  6.65 us
    unnamed x45, local copies, waits for them, and re-layouts  6.56 us
  transfers between devices with their start and end apart: 6, of which 4 were waited for; matrix products, arithmetic and copies ran while one was open for 21% of the time, Pallas kernels for 0%

commit v1 on v0

v1 whole, which is shorter than its diff:
```python
import jax
import jax.numpy as jnp
from jax import lax
from jax.experimental import pallas as pl
from jax.experimental.pallas import tpu as pltpu
from jax.sharding import PartitionSpec as P

DZ = 64
OVL = 6
CELLS = 1280
HALO = 3
CHUNK = 16


e_half = 4.5
centre = 5.0
sigma_one = e_half / (-3.5 - centre)
sigma_two = 1.0 / (2.0 / sigma_one - sigma_one)
sigma_three = 1.0 / (2.0 / sigma_one - sigma_two)
rashba = 0.3

ALPHA1 = sigma_one / e_half
ALPHA2 = 2.0 * sigma_two / e_half
BETA2 = -sigma_one * sigma_two
ALPHA3 = 2.0 * sigma_three / e_half
BETA3 = -sigma_two * sigma_three
RH = 0.5 * rashba


def _make_kernel(planes, chunk, aliased):
    rows_n = chunk // 8

    def kernel(valid_ref, f_ref, lo_ref, cur_ref, hi_ref, *rest):
        if aliased:
            out_ref, y1_ref, y2_ref = rest[1:]
        else:
            out_ref, y1_ref, y2_ref = rest
        cell = lax.broadcasted_iota(jnp.int32, (8, CELLS), 1)
        zc = cell % DZ
        m_yn = cell < CELLS - DZ
        m_yp = cell >= DZ
        m_zn = zc != DZ - 1
        m_zp = zc != 0

        def band(q, k, rows):
            if q < 0:
                return lo_ref[k, q + HALO, rows, :]
            if q < planes:
                return cur_ref[k, q, rows, :]
            return hi_ref[k, q - planes, rows, :]

        def from_y1(q, k, rows):
            return y1_ref[k, q + 2, rows, :]

        def from_y2(q, k, rows):
            return y2_ref[k, q + 1, rows, :]

        def apply(src, q, rows):
            d_up = f_ref[0, q + 2 : q + 3, :]
            d_dn = f_ref[1, q + 2 : q + 3, :]
            bx = f_ref[2, q + 2 : q + 3, :]
            by = f_ref[3, q + 2 : q + 3, :]
            o = [None] * 4

            def add(i, v):
                o[i] = v if o[i] is None else o[i] + v

            for k in range(4):
                m = src(q, k, rows)
                xn = src(q + 1, k, rows)
                xp = src(q - 1, k, rows)
                yn = jnp.where(m_yn, pltpu.roll(m, CELLS - DZ, 1), 0.0)
                yp = jnp.where(m_yp, pltpu.roll(m, DZ, 1), 0.0)
                zn = jnp.where(m_zn, pltpu.roll(m, CELLS - 1, 1), 0.0)
                zp = jnp.where(m_zp, pltpu.roll(m, 1, 1), 0.0)
                nb = (xn + xp) + (yn + yp) + (zn + zp)
                dx = RH * (xn - xp)
                dy = RH * (yn - yp)
                if k == 0:
                    add(0, d_up * m - 0.5 * nb)
                    add(2, bx * m - dx)
                    add(3, by * m - dy)
                elif k == 1:
                    add(1, d_up * m - 0.5 * nb)
                    add(2, dy - by * m)
                    add(3, bx * m - dx)
                elif k == 2:
                    add(2, d_dn * m - 0.5 * nb)
                    add(0, bx * m + dx)
                    add(1, -(by * m) - dy)
                else:
                    add(3, d_dn * m - 0.5 * nb)
                    add(0, by * m + dy)
                    add(1, bx * m + dx)
            return o

        def run_stage(src, dst, prev, q_lo, q_hi, alpha, beta):
            for q in range(q_lo, q_hi):
                halo_plane = q < 0 or q >= planes

                def body(r, carry, q=q, halo_plane=halo_plane):
                    rows = pl.ds(pl.multiple_of(r * 8, 8), 8)
                    o = apply(src, q, rows)
                    scale = valid_ref[q + HALO] if halo_plane else None
                    for k in range(4):
                        res = alpha * o[k]
                        if prev is not None:
                            res = res + beta * prev(q, k, rows)
                        if scale is not None:
                            res = res * scale
                        dst(q, k, rows, res)
                    return carry

                lax.fori_loop(0, rows_n, body, 0)

        def put_y1(q, k, rows, v):
            y1_ref[k, q + 2, rows, :] = v

        def put_y2(q, k, rows, v):
            y2_ref[k, q + 1, rows, :] = v

        def put_out(q, k, rows, v):
            out_ref[k, q, rows, :] = v

        run_stage(band, put_y1, None, -2, planes + 2, ALPHA1, 0.0)
        run_stage(from_y1, put_y2, band, -1, planes + 1, ALPHA2, BETA2)
        run_stage(from_y2, put_out, from_y1, 0, planes, ALPHA3, BETA3)

    return kernel


def _filter_chunk(valid, fext, lo, cur_full, hi, acc, c, planes, chunk):
    aliased = acc is not None
    nb_full = cur_full.shape[2]
    blk = (4, HALO, chunk, CELLS)
    in_specs = [
        pl.BlockSpec(memory_space=pltpu.SMEM),
        pl.BlockSpec(fext.shape, lambda i: (0, 0, 0)),
        pl.BlockSpec(blk, lambda i: (0, 0, 0, 0)),
        pl.BlockSpec((4, planes, chunk, CELLS), lambda i: (0, 0, c, 0)),
        pl.BlockSpec(blk, lambda i: (0, 0, 0, 0)),
    ]
    args = [valid, fext, lo, cur_full, hi]
    extra = {}
    if aliased:
        in_specs.append(pl.BlockSpec(memory_space=pl.ANY))
        args.append(acc)
        extra["input_output_aliases"] = {5: 0}
    return pl.pallas_call(
        _make_kernel(planes, chunk, aliased),
        grid=(1,),
        in_specs=in_specs,
        out_specs=pl.BlockSpec((4, planes, chunk, CELLS), lambda i: (0, 0, c, 0)),
        out_shape=jax.ShapeDtypeStruct((4, planes, nb_full, CELLS), jnp.float32),
        scratch_shapes=[
            pltpu.VMEM((4, planes + 4, chunk, CELLS), jnp.float32),
            pltpu.VMEM((4, planes + 2, chunk, CELLS), jnp.float32),
        ],
        compiler_params=pltpu.CompilerParams(vmem_limit_bytes=48 * 1024 * 1024),
        **extra,
    )(*args)


def _shift(x, axis, step):
    count = lax.axis_size(axis)
    if step > 0:
        pairs = [(i, i + 1) for i in range(count - 1)]
    else:
        pairs = [(i + 1, i) for i in range(count - 1)]
    return lax.ppermute(x, axis, pairs)


def _fields(potential, domain_blocks, block_slots, domain_offsets):
    ndom = lax.axis_size("dom")
    per_dev = potential.shape[2]
    planes = potential.shape[1]
    d = lax.axis_index("dom")
    slot_of = block_slots[domain_blocks]

    def local_for(t):
        slots_t = slot_of[t]
        match = (slots_t // per_dev) == d
        return jnp.sum(jnp.where(match, slots_t % per_dev, 0))

    recv = []
    for k in range(ndom):
        t = (d + k) % ndom
        send = lax.dynamic_index_in_dim(potential, local_for(t), axis=2, keepdims=False)
        if k == 0:
            recv.append(send)
        else:
            recv.append(lax.ppermute(send, "dom", [(i, (i + k) % ndom) for i in range(ndom)]))
    allr = jnp.stack(recv)
    mine = slot_of[d]
    ks = (d - mine // per_dev) % ndom
    blocks = jnp.take(allr, ks, axis=0)
    window = jnp.transpose(blocks, (1, 2, 0, 3)).reshape(4, planes, OVL * potential.shape[3])
    f = lax.dynamic_slice_in_dim(window, domain_offsets[d] * DZ, CELLS, 2)
    v, bx, by, bz = f[0], f[1], f[2], f[3]
    return jnp.stack([v + bz + (3.0 - centre), v - bz + (3.0 - centre), bx, by])


def per_device(bands, potential, domain_blocks, block_slots, domain_offsets):
    b = jnp.transpose(bands[0], (0, 2, 1, 3))
    planes = b.shape[1]
    nbands = b.shape[2]
    g = lax.axis_index("grid")
    ng = lax.axis_size("grid")
    chunk = CHUNK

    los, his = [], []
    for c in range(nbands // chunk):
        bc = b[:, :, c * chunk : (c + 1) * chunk]
        los.append(_shift(bc[:, planes - HALO :], "grid", 1))
        his.append(_shift(bc[:, :HALO], "grid", -1))

    f = _fields(potential, domain_blocks, block_slots, domain_offsets)
    f_lo = _shift(f[:, planes - 2 :], "grid", 1)
    f_hi = _shift(f[:, :2], "grid", -1)
    fext = jnp.concatenate([f_lo, f, f_hi], axis=1)

    q = jnp.arange(-HALO, planes + HALO)
    glob = g * planes + q
    valid = ((glob >= 0) & (glob < ng * planes)).astype(jnp.float32)

    acc = None
    for c in range(nbands // chunk):
        acc = _filter_chunk(valid, fext, los[c], b, his[c], acc, c, planes, chunk)
    return jnp.transpose(acc, (0, 2, 1, 3))[None]


def solution(mesh):
    placed = (P("dom", None, None, "grid", None), P(None, "grid", "dom", None), P(), P(), P())
    return jax.shard_map(
        per_device,
        mesh=mesh,
        in_specs=placed,
        out_specs=P("dom", None, None, "grid", None),
        check_vma=False,
    )
```

time: 171 us -> 122 us (0.71)
  other arithmetic: 53 us -> 1.18 us
  Pallas kernels: 0 us -> 38.2 us
  local copies, waits for them, and re-layouts: 44.6 us -> 8.75 us
  blocking collectives: 28.8 us -> 0 us
  starting transfers between devices: 24.2 us -> 51.3 us
  between operations: 1.01 us -> 16.2 us
  waiting for transfers between devices: 19.4 us -> 5.18 us
    pallas_call x0 -> x4, Pallas kernels: none -> 38.2 us  [_filter_chunk(): pl.pallas_call(_make_kernel(planes, chunk, aliased), grid=(1,), in_specs=...]
    sub x5 -> x0, other arithmetic: 34.1 us -> none  [the longest x3 28.5 us: apply_h(): lapl = x_next + x_prev + y_next + y_prev + z_next + z_prev - 6.0 * middle]
    slice x10 -> x3, local copies, waits for them, and re-layouts: 35.7 us -> 4.24 us  [the longest x1 4.12 us: per_device(): bc = b[:, :, c * chunk:(c + 1) * chunk]]
    all_gather x1 -> x0, blocking collectives: 28.8 us -> none  [per_device(): gathered = lax.all_gather(potential, 'dom', axis=2, tiled=True)]
    ppermute x6 -> x17, starting transfers between devices: 24.2 us -> 51.3 us  [the longest x10 36.6 us: _shift(): return lax.ppermute(x, axis, pairs)]
    ppermute x6 -> x17, waiting for transfers between devices: 19.4 us -> 5.18 us  [the longest x10 5.16 us: _shift(): return lax.ppermute(x, axis, pairs)]
    add x4 -> x1, other arithmetic: 9.6 us -> 0.09 us  [_fields(): return jnp.stack([v + bz + (3.0 - centre), v - bz + (3.0 - centre), bx, by])]
    another operation x2 -> x1, other arithmetic: 6.03 us -> 0.02 us  [_fields(): return jnp.stack([v + bz + (3.0 - centre), v - bz + (3.0 - centre), bx, by])]
  transfers between devices with their start and end apart: 6 -> 17, of which waited for: 4 -> 1; matrix products, arithmetic and copies ran while one was open for 21% -> 3% of each run, Pallas kernels for 0% -> 23%
where the time goes in v1:
time: 122 us; the launch traced here: 121 us
  starting transfers between devices  51.3 us (42%)
  Pallas kernels  38.2 us (31%)
  between operations  16.2 us (13%)
  local copies, waits for them, and re-layouts  8.75 us (7%)
  waiting for transfers between devices  5.18 us (4%)
    pallas_call x4, Pallas kernels, _filter_chunk(): pl.pallas_call(_make_kernel(planes, chunk, aliased), grid=(1,), in_specs=...  38.2 us
    ppermute x10, starting transfers between devices, _shift(): return lax.ppermute(x, axis, pairs)  36.6 us
    ppermute x7, starting transfers between devices, _fields(): lax.ppermute(send, 'dom', [(i, (i + k) % ndom) for i in range(ndom)])  14.7 us
    ppermute x10, waiting for transfers between devices, _shift(): return lax.ppermute(x, axis, pairs)  5.16 us
    slice x1, local copies, waits for them, and re-layouts, per_device(): bc = b[:, :, c * chunk:(c + 1) * chunk]  4.12 us
  transfers between devices with their start and end apart: 17, of which 1 were waited for; matrix products, arithmetic and copies ran while one was open for 3% of the time, Pallas kernels for 23%

profile of v1, /device:TPU:25, one launch (start us, length us, event | category | flops | bytes accessed | tf_op | source)
XLA Modules:
  0.0 120.8 jit_solution(13667103845354319045)
XLA Ops:
  0.0 4.1 %fusion.19 = (f32[4,3,16,1280]{3,2,1,0:T(8,128)}, f32[4,3,16,1280]{3,2,1,0:T(8,128)}, f32[4,3,16,1280]{3,2,1,0:T(8,128)}, f32[4,3,16,1280]{3,2,1,0:T(8,128)}) fusion(f32[4,3,64,1280]{3,2,1,0:T(8,128)} %bitcast.116), kind=kLoop, calls=%fused_computation.130 | loop fusion | bytes 7864320 | tf_op jit(solution)/shard_map/slice | solution.py:213
  4.1 3.9 %collective-permute-start.15 = (f32[4,3,16,1280]{3,2,1,0:T(8,128)}, f32[4,3,16,1280]{3,2,1,0:T(8,128)S(1)}, u32[]{:S(2)}, u32[]{:S(2)}) collective-permute-start(f32[4,3,16,1280]{3,2,1,0:T(8,128)} %get-tuple-element.13), channel_id=1, source_target_pairs={{0,1},{1,2},{2,3},{3,4},{4,5},{5,6},{6,7},{7,8},{8,9},{9,10},{10,1... | collective-permute-start | bytes 2949128 | tf_op jit(solution)/shard_map/ppermute | solution.py:170
  8.0 1.9 %collective-permute-start.16 = (f32[4,3,16,1280]{3,2,1,0:T(8,128)}, f32[4,3,16,1280]{3,2,1,0:T(8,128)S(1)}, u32[]{:S(2)}, u32[]{:S(2)}) collective-permute-start(f32[4,3,16,1280]{3,2,1,0:T(8,128)} %get-tuple-element.13), channel_id=1, source_target_pairs={{1,0},{2,1},{3,2},{4,3},{5,4},{6,5},{7,6},{8,7},{9,8},{10,9},{11,1... | collective-permute-start | bytes 2949128 | tf_op jit(solution)/shard_map/ppermute | solution.py:170
  27.1 3.4 %collective-permute-start = (f32[4,3,256]{2,0,1:T(4,128)S(1)}, f32[4,3,256]{2,0,1:T(4,128)S(1)}, u32[]{:S(2)}, u32[]{:S(2)}) collective-permute-start(f32[4,3,256]{2,0,1:T(4,128)S(1)} %bitcast.127), channel_id=1, source_target_pairs={{0,16},{16,32},{32,48},{48,64},{64,80},{80,96},{96,112},{112,0},{1... | collective-permute-start | bytes 36872 | tf_op jit(solution)/shard_map/ppermute | solution.py:192
  30.5 1.2 %collective-permute-start.1 = (f32[4,3,256]{2,0,1:T(4,128)S(1)}, f32[4,3,256]{2,0,1:T(4,128)S(1)}, u32[]{:S(2)}, u32[]{:S(2)}) collective-permute-start(f32[4,3,256]{2,0,1:T(4,128)S(1)} %bitcast.125), channel_id=1, source_target_pairs={{0,32},{16,48},{32,64},{48,80},{64,96},{80,112},{96,0},{112,16},{1... | collective-permute-start | bytes 36872 | tf_op jit(solution)/shard_map/ppermute | solution.py:192
  31.7 1.2 %collective-permute-start.2 = (f32[4,3,256]{2,0,1:T(4,128)S(1)}, f32[4,3,256]{2,0,1:T(4,128)S(1)}, u32[]{:S(2)}, u32[]{:S(2)}) collective-permute-start(f32[4,3,256]{2,0,1:T(4,128)S(1)} %bitcast.124), channel_id=1, source_target_pairs={{0,48},{16,64},{32,80},{48,96},{64,112},{80,0},{96,16},{112,32},{1... | collective-permute-start | bytes 36872 | tf_op jit(solution)/shard_map/ppermute | solution.py:192
  34.3 1.8 %collective-permute-start.3 = (f32[4,3,256]{2,0,1:T(4,128)S(1)}, f32[4,3,256]{2,0,1:T(4,128)S(1)}, u32[]{:S(2)}, u32[]{:S(2)}) collective-permute-start(f32[4,3,256]{2,0,1:T(4,128)S(1)} %bitcast.126), channel_id=1, source_target_pairs={{0,64},{16,80},{32,96},{48,112},{64,0},{80,16},{96,32},{112,48},{1... | collective-permute-start | bytes 36872 | tf_op jit(solution)/shard_map/ppermute | solution.py:192
  36.1 4.9 %collective-permute-start.4 = (f32[4,3,256]{2,0,1:T(4,128)S(1)}, f32[4,3,256]{2,0,1:T(4,128)S(1)}, u32[]{:S(2)}, u32[]{:S(2)}) collective-permute-start(f32[4,3,256]{2,0,1:T(4,128)S(1)} %bitcast.123), channel_id=1, source_target_pairs={{0,80},{16,96},{32,112},{48,0},{64,16},{80,32},{96,48},{112,64},{1... | collective-permute-start | bytes 36872 | tf_op jit(solution)/shard_map/ppermute | solution.py:192
  41.0 1.2 collective-permute-start.5
  42.2 1.0 collective-permute-start.6
  43.2 7.4 %collective-permute-start.13 = (f32[4,3,16,1280]{3,2,1,0:T(8,128)}, f32[4,3,16,1280]{3,2,1,0:T(8,128)S(1)}, u32[]{:S(2)}, u32[]{:S(2)}) collective-permute-start(f32[4,3,16,1280]{3,2,1,0:T(8,128)} %get-tuple-element.14), channel_id=1, source_target_pairs={{0,1},{1,2},{2,3},{3,4},{4,5},{5,6},{6,7},{7,8},{8,9},{9,10},{10,1... | collective-permute-start | bytes 2949128 | tf_op jit(solution)/shard_map/ppermute | solution.py:170
  51.7 3.5 %collective-permute-start.7 = (f32[4,2,1280]{2,1,0:T(2,128)S(1)}, f32[4,2,1280]{2,1,0:T(2,128)S(1)}, u32[]{:S(2)}, u32[]{:S(2)}) collective-permute-start(f32[4,2,1280]{2,1,0:T(2,128)S(1)} %get-tuple-element.19), channel_id=1, source_target_pairs={{0,1},{1,2},{2,3},{3,4},{4,5},{5,6},{6,7},{7,8},{8,9},{9,10},{10,1... | collective-permute-start | bytes 122888 | tf_op jit(solution)/shard_map/ppermute | solution.py:170
  55.2 1.9 %collective-permute-start.8 = (f32[4,2,1280]{2,1,0:T(2,128)S(1)}, f32[4,2,1280]{2,1,0:T(2,128)S(1)}, u32[]{:S(2)}, u32[]{:S(2)}) collective-permute-start(f32[4,2,1280]{2,1,0:T(2,128)S(1)} %get-tuple-element.20), channel_id=1, source_target_pairs={{1,0},{2,1},{3,2},{4,3},{5,4},{6,5},{7,6},{8,7},{9,8},{10,9},{11,1... | collective-permute-start | bytes 122888 | tf_op jit(solution)/shard_map/ppermute | solution.py:170
  57.2 5.1 %collective-permute-done.7 = f32[4,2,1280]{2,1,0:T(2,128)S(1)} collective-permute-done((f32[4,2,1280]{2,1,0:T(2,128)S(1)}, f32[4,2,1280]{2,1,0:T(2,128)S(1)}, u32[]{:S(2)}, u32[]{:S(2)}) %collective-permute-start.7) | collective-permute-done | bytes 40992 | tf_op jit(solution)/shard_map/ppermute | solution.py:170
  62.3 2.0 %collective-permute-start.14 = (f32[4,3,16,1280]{3,2,1,0:T(8,128)}, f32[4,3,16,1280]{3,2,1,0:T(8,128)}, u32[]{:S(2)}, u32[]{:S(2)}) collective-permute-start(f32[4,3,16,1280]{3,2,1,0:T(8,128)} %get-tuple-element.14), channel_id=1, source_target_pairs={{1,0},{2,1},{3,2},{4,3},{5,4},{6,5},{7,6},{8,7},{9,8},{10,9},{11,1... | collective-permute-start | bytes 2949128 | tf_op jit(solution)/shard_map/ppermute | solution.py:170
  64.3 6.4 %collective-permute-start.11 = (f32[4,3,16,1280]{3,2,1,0:T(8,128)}, f32[4,3,16,1280]{3,2,1,0:T(8,128)}, u32[]{:S(2)}, u32[]{:S(2)}) collective-permute-start(f32[4,3,16,1280]{3,2,1,0:T(8,128)} %get-tuple-element.15), channel_id=1, source_target_pairs={{0,1},{1,2},{2,3},{3,4},{4,5},{5,6},{6,7},{7,8},{8,9},{9,10},{10,1... | collective-permute-start | bytes 2949128 | tf_op jit(solution)/shard_map/ppermute | solution.py:170
  70.8 1.9 %collective-permute-start.12 = (f32[4,3,16,1280]{3,2,1,0:T(8,128)}, f32[4,3,16,1280]{3,2,1,0:T(8,128)}, u32[]{:S(2)}, u32[]{:S(2)}) collective-permute-start(f32[4,3,16,1280]{3,2,1,0:T(8,128)} %get-tuple-element.15), channel_id=1, source_target_pairs={{1,0},{2,1},{3,2},{4,3},{5,4},{6,5},{7,6},{8,7},{9,8},{10,9},{11,1... | collective-permute-start | bytes 2949128 | tf_op jit(solution)/shard_map/ppermute | solution.py:170
  72.7 1.9 %collective-permute-start.10 = (f32[4,3,16,1280]{3,2,1,0:T(8,128)}, f32[4,3,16,1280]{3,2,1,0:T(8,128)}, u32[]{:S(2)}, u32[]{:S(2)}) collective-permute-start(f32[4,3,16,1280]{3,2,1,0:T(8,128)} %get-tuple-element.16), channel_id=1, source_target_pairs={{1,0},{2,1},{3,2},{4,3},{5,4},{6,5},{7,6},{8,7},{9,8},{10,9},{11,1... | collective-permute-start | bytes 2949128 | tf_op jit(solution)/shard_map/ppermute | solution.py:170
  74.6 5.8 %collective-permute-start.9 = (f32[4,3,16,1280]{3,2,1,0:T(8,128)}, f32[4,3,16,1280]{3,2,1,0:T(8,128)}, u32[]{:S(2)}, u32[]{:S(2)}) collective-permute-start(f32[4,3,16,1280]{3,2,1,0:T(8,128)} %get-tuple-element.16), channel_id=1, source_target_pairs={{0,1},{1,2},{2,3},{3,4},{4,5},{5,6},{6,7},{7,8},{8,9},{9,10},{10,1... | collective-permute-start | bytes 2949128 | tf_op jit(solution)/shard_map/ppermute | solution.py:170
  80.5 2.1 %copy-done.1 = f32[1,4,64,3,1280]{4,2,3,1,0:T(8,128)S(1)} copy-done((f32[1,4,64,3,1280]{4,2,3,1,0:T(8,128)S(1)}, f32[1,4,64,3,1280]{4,2,3,1,0:T(8,128)}, u32[]{:S(2)}) %copy-start.1) | copy-done | bytes 3932184
  82.6 9.0 %shard_map.55.rest_0_ = f32[4,3,64,1280]{3,2,1,0:T(8,128)} custom-call(f32[9]{0:T(128)S(1)} %and_convert_fusion.valid_ref, f32[4,7,1280]{2,1,0:T(8,128)S(1)} %pad_maximum_fusion.f_ref, f32[4,3,16,1280]{3,2,1,0:T(8,128)S(1)} %collective-permute-done.15.lo_ref, f32[4,3,64,1280]{3,2,1,0:T(8,128)S(1)} %bitcast.117, ...), custom_call_target="tpu_custom_call" | custom-call | tf_op jit(solution)/shard_map/pallas_call | solution.py:149
  91.6 9.6 %shard_map.56.rest_0_ = f32[4,3,64,1280]{3,2,1,0:T(8,128)} custom-call(f32[9]{0:T(128)S(1)} %and_convert_fusion.valid_ref, f32[4,7,1280]{2,1,0:T(8,128)S(1)} %pad_maximum_fusion.f_ref, f32[4,3,16,1280]{3,2,1,0:T(8,128)S(1)} %collective-permute-done.13.lo_ref, f32[4,3,64,1280]{3,2,1,0:T(8,128)S(1)} %bitcast.118, ...), custom_call_target="tpu_custom_call", output_to_operand_aliasing={{}: (5, {})} | custom-call | tf_op jit(solution)/shard_map/pallas_call | solution.py:149
  101.2 9.8 %shard_map.57.rest_0_ = f32[4,3,64,1280]{3,2,1,0:T(8,128)} custom-call(f32[9]{0:T(128)S(1)} %and_convert_fusion.valid_ref, f32[4,7,1280]{2,1,0:T(8,128)S(1)} %pad_maximum_fusion.f_ref, f32[4,3,16,1280]{3,2,1,0:T(8,128)} %collective-permute-done.11.lo_ref, f32[4,3,64,1280]{3,2,1,0:T(8,128)S(1)} %bitcast.119, ...), custom_call_target="tpu_custom_call", output_to_operand_aliasing={{}: (5, {})} | custom-call | tf_op jit(solution)/shard_map/pallas_call | solution.py:149
  111.0 9.8 %shard_map.58 = f32[4,3,64,1280]{3,2,1,0:T(8,128)} custom-call(f32[9]{0:T(128)S(1)} %and_convert_fusion.valid_ref, f32[4,7,1280]{2,1,0:T(8,128)S(1)} %pad_maximum_fusion.f_ref, f32[4,3,16,1280]{3,2,1,0:T(8,128)} %collective-permute-done.9.lo_ref, f32[4,3,64,1280]{3,2,1,0:T(8,128)S(1)} %bitcast.120, ...), custom_call_target="tpu_custom_call", output_to_operand_aliasing={{}: (5, {})} | custom-call | tf_op jit(solution)/shard_map/pallas_call | solution.py:149
  (63 shorter events, 3.7 us)
Async XLA Ops:
  0.0 10.2 %copy-start = (s32[32]{0:T(128)S(1)}, s32[32]{0:T(128)}, u32[]{:S(2)}) copy-start(s32[32]{0:T(128)} %param.8) | copy-start | bytes 388
  0.0 10.1 %copy-start.4 = (s32[8,6]{1,0:T(8,128)S(1)}, s32[8,6]{1,0:T(8,128)}, u32[]{:S(2)}) copy-start(s32[8,6]{1,0:T(8,128)} %param.7) | copy-start | bytes 580
  4.1 22.9 %copy-start.3 = (f32[4,3,4,256]{3,2,1,0:T(4,128)S(1)}, f32[4,3,4,256]{3,2,1,0:T(4,128)}, u32[]{:S(2)}) copy-start(f32[4,3,4,256]{3,2,1,0:T(4,128)} %param.6) | copy-start | bytes 147460
  4.1 28.9 %copy-start.5 = (s32[8]{0:T(128)S(1)}, s32[8]{0:T(128)}, u32[]{:S(2)}) copy-start(s32[8]{0:T(128)} %param.9) | copy-start | bytes 100
  4.1 66.6 %collective-permute-start.15 = (f32[4,3,16,1280]{3,2,1,0:T(8,128)}, f32[4,3,16,1280]{3,2,1,0:T(8,128)S(1)}, u32[]{:S(2)}, u32[]{:S(2)}) collective-permute-start(f32[4,3,16,1280]{3,2,1,0:T(8,128)} %get-tuple-element.13), channel_id=1, source_target_pairs={{0,1},{1,2},{2,3},{3,4},{4,5},{5,6},{6,7},{7,8},{8,9},{9,10},{10,1... | collective-permute-start | bytes 2949128 | tf_op jit(solution)/shard_map/ppermute | solution.py:170
  8.0 64.7 %collective-permute-start.16 = (f32[4,3,16,1280]{3,2,1,0:T(8,128)}, f32[4,3,16,1280]{3,2,1,0:T(8,128)S(1)}, u32[]{:S(2)}, u32[]{:S(2)}) collective-permute-start(f32[4,3,16,1280]{3,2,1,0:T(8,128)} %get-tuple-element.13), channel_id=1, source_target_pairs={{1,0},{2,1},{3,2},{4,3},{5,4},{6,5},{7,6},{8,7},{9,8},{10,9},{11,1... | collective-permute-start | bytes 2949128 | tf_op jit(solution)/shard_map/ppermute | solution.py:170
  27.1 7.2 %collective-permute-start = (f32[4,3,256]{2,0,1:T(4,128)S(1)}, f32[4,3,256]{2,0,1:T(4,128)S(1)}, u32[]{:S(2)}, u32[]{:S(2)}) collective-permute-start(f32[4,3,256]{2,0,1:T(4,128)S(1)} %bitcast.127), channel_id=1, source_target_pairs={{0,16},{16,32},{32,48},{48,64},{64,80},{80,96},{96,112},{112,0},{1... | collective-permute-start | bytes 36872 | tf_op jit(solution)/shard_map/ppermute | solution.py:192
  30.5 5.6 %collective-permute-start.1 = (f32[4,3,256]{2,0,1:T(4,128)S(1)}, f32[4,3,256]{2,0,1:T(4,128)S(1)}, u32[]{:S(2)}, u32[]{:S(2)}) collective-permute-start(f32[4,3,256]{2,0,1:T(4,128)S(1)} %bitcast.125), channel_id=1, source_target_pairs={{0,32},{16,48},{32,64},{48,80},{64,96},{80,112},{96,0},{112,16},{1... | collective-permute-start | bytes 36872 | tf_op jit(solution)/shard_map/ppermute | solution.py:192
  31.7 9.3 %collective-permute-start.2 = (f32[4,3,256]{2,0,1:T(4,128)S(1)}, f32[4,3,256]{2,0,1:T(4,128)S(1)}, u32[]{:S(2)}, u32[]{:S(2)}) collective-permute-start(f32[4,3,256]{2,0,1:T(4,128)S(1)} %bitcast.124), channel_id=1, source_target_pairs={{0,48},{16,64},{32,80},{48,96},{64,112},{80,0},{96,16},{112,32},{1... | collective-permute-start | bytes 36872 | tf_op jit(solution)/shard_map/ppermute | solution.py:192
  34.3 7.9 %collective-permute-start.3 = (f32[4,3,256]{2,0,1:T(4,128)S(1)}, f32[4,3,256]{2,0,1:T(4,128)S(1)}, u32[]{:S(2)}, u32[]{:S(2)}) collective-permute-start(f32[4,3,256]{2,0,1:T(4,128)S(1)} %bitcast.126), channel_id=1, source_target_pairs={{0,64},{16,80},{32,96},{48,112},{64,0},{80,16},{96,32},{112,48},{1... | collective-permute-start | bytes 36872 | tf_op jit(solution)/shard_map/ppermute | solution.py:192
  36.1 7.1 %collective-permute-start.4 = (f32[4,3,256]{2,0,1:T(4,128)S(1)}, f32[4,3,256]{2,0,1:T(4,128)S(1)}, u32[]{:S(2)}, u32[]{:S(2)}) collective-permute-start(f32[4,3,256]{2,0,1:T(4,128)S(1)} %bitcast.123), channel_id=1, source_target_pairs={{0,80},{16,96},{32,112},{48,0},{64,16},{80,32},{96,48},{112,64},{1... | collective-permute-start | bytes 36872 | tf_op jit(solution)/shard_map/ppermute | solution.py:192
  41.0 9.6 %collective-permute-start.5 = (f32[4,3,256]{2,0,1:T(4,128)S(1)}, f32[4,3,256]{2,0,1:T(4,128)S(1)}, u32[]{:S(2)}, u32[]{:S(2)}) collective-permute-start(f32[4,3,256]{2,0,1:T(4,128)S(1)} %bitcast.122), channel_id=1, source_target_pairs={{0,96},{16,112},{32,0},{48,16},{64,32},{80,48},{96,64},{112,80},{1... | collective-permute-start | bytes 36872 | tf_op jit(solution)/shard_map/ppermute | solution.py:192
  42.2 8.5 %collective-permute-start.6 = (f32[4,3,256]{2,0,1:T(4,128)S(1)}, f32[4,3,256]{2,0,1:T(4,128)S(1)}, u32[]{:S(2)}, u32[]{:S(2)}) collective-permute-start(f32[4,3,256]{2,0,1:T(4,128)S(1)} %bitcast.121), channel_id=1, source_target_pairs={{0,112},{16,0},{32,16},{48,32},{64,48},{80,64},{96,80},{112,96},{1... | collective-permute-start | bytes 36872 | tf_op jit(solution)/shard_map/ppermute | solution.py:192
  43.2 31.4 %collective-permute-start.13 = (f32[4,3,16,1280]{3,2,1,0:T(8,128)}, f32[4,3,16,1280]{3,2,1,0:T(8,128)S(1)}, u32[]{:S(2)}, u32[]{:S(2)}) collective-permute-start(f32[4,3,16,1280]{3,2,1,0:T(8,128)} %get-tuple-element.14), channel_id=1, source_target_pairs={{0,1},{1,2},{2,3},{3,4},{4,5},{5,6},{6,7},{7,8},{8,9},{9,10},{10,1... | collective-permute-start | bytes 2949128 | tf_op jit(solution)/shard_map/ppermute | solution.py:170
  51.7 10.6 %collective-permute-start.7 = (f32[4,2,1280]{2,1,0:T(2,128)S(1)}, f32[4,2,1280]{2,1,0:T(2,128)S(1)}, u32[]{:S(2)}, u32[]{:S(2)}) collective-permute-start(f32[4,2,1280]{2,1,0:T(2,128)S(1)} %get-tuple-element.19), channel_id=1, source_target_pairs={{0,1},{1,2},{2,3},{3,4},{4,5},{5,6},{6,7},{7,8},{8,9},{9,10},{10,1... | collective-permute-start | bytes 122888 | tf_op jit(solution)/shard_map/ppermute | solution.py:170
  55.2 9.1 %collective-permute-start.8 = (f32[4,2,1280]{2,1,0:T(2,128)S(1)}, f32[4,2,1280]{2,1,0:T(2,128)S(1)}, u32[]{:S(2)}, u32[]{:S(2)}) collective-permute-start(f32[4,2,1280]{2,1,0:T(2,128)S(1)} %get-tuple-element.20), channel_id=1, source_target_pairs={{1,0},{2,1},{3,2},{4,3},{5,4},{6,5},{7,6},{8,7},{9,8},{10,9},{11,1... | collective-permute-start | bytes 122888 | tf_op jit(solution)/shard_map/ppermute | solution.py:170
  62.3 29.3 %collective-permute-start.14 = (f32[4,3,16,1280]{3,2,1,0:T(8,128)}, f32[4,3,16,1280]{3,2,1,0:T(8,128)}, u32[]{:S(2)}, u32[]{:S(2)}) collective-permute-start(f32[4,3,16,1280]{3,2,1,0:T(8,128)} %get-tuple-element.14), channel_id=1, source_target_pairs={{1,0},{2,1},{3,2},{4,3},{5,4},{6,5},{7,6},{8,7},{9,8},{10,9},{11,1... | collective-permute-start | bytes 2949128 | tf_op jit(solution)/shard_map/ppermute | solution.py:170
  64.3 36.9 %collective-permute-start.11 = (f32[4,3,16,1280]{3,2,1,0:T(8,128)}, f32[4,3,16,1280]{3,2,1,0:T(8,128)}, u32[]{:S(2)}, u32[]{:S(2)}) collective-permute-start(f32[4,3,16,1280]{3,2,1,0:T(8,128)} %get-tuple-element.15), channel_id=1, source_target_pairs={{0,1},{1,2},{2,3},{3,4},{4,5},{5,6},{6,7},{7,8},{8,9},{9,10},{10,1... | collective-permute-start | bytes 2949128 | tf_op jit(solution)/shard_map/ppermute | solution.py:170
  70.8 30.4 %collective-permute-start.12 = (f32[4,3,16,1280]{3,2,1,0:T(8,128)}, f32[4,3,16,1280]{3,2,1,0:T(8,128)}, u32[]{:S(2)}, u32[]{:S(2)}) collective-permute-start(f32[4,3,16,1280]{3,2,1,0:T(8,128)} %get-tuple-element.15), channel_id=1, source_target_pairs={{1,0},{2,1},{3,2},{4,3},{5,4},{6,5},{7,6},{8,7},{9,8},{10,9},{11,1... | collective-permute-start | bytes 2949128 | tf_op jit(solution)/shard_map/ppermute | solution.py:170
  72.7 38.3 %collective-permute-start.10 = (f32[4,3,16,1280]{3,2,1,0:T(8,128)}, f32[4,3,16,1280]{3,2,1,0:T(8,128)}, u32[]{:S(2)}, u32[]{:S(2)}) collective-permute-start(f32[4,3,16,1280]{3,2,1,0:T(8,128)} %get-tuple-element.16), channel_id=1, source_target_pairs={{1,0},{2,1},{3,2},{4,3},{5,4},{6,5},{7,6},{8,7},{9,8},{10,9},{11,1... | collective-permute-start | bytes 2949128 | tf_op jit(solution)/shard_map/ppermute | solution.py:170
  74.6 36.3 %collective-permute-start.9 = (f32[4,3,16,1280]{3,2,1,0:T(8,128)}, f32[4,3,16,1280]{3,2,1,0:T(8,128)}, u32[]{:S(2)}, u32[]{:S(2)}) collective-permute-start(f32[4,3,16,1280]{3,2,1,0:T(8,128)} %get-tuple-element.16), channel_id=1, source_target_pairs={{0,1},{1,2},{2,3},{3,4},{4,5},{5,6},{6,7},{7,8},{8,9},{9,10},{10,1... | collective-permute-start | bytes 2949128 | tf_op jit(solution)/shard_map/ppermute | solution.py:170
  80.5 2.1 %copy-start.1 = (f32[1,4,64,3,1280]{4,2,3,1,0:T(8,128)S(1)}, f32[1,4,64,3,1280]{4,2,3,1,0:T(8,128)}, u32[]{:S(2)}) copy-start(f32[1,4,64,3,1280]{4,2,3,1,0:T(8,128)} %param.5) | copy-start | bytes 11796484
  82.6 9.0 %copy-start.2 = (f32[1,4,64,3,1280]{4,2,3,1,0:T(8,128)S(1)}, f32[1,4,64,3,1280]{4,2,3,1,0:T(8,128)}, u32[]{:S(2)}) copy-start(f32[1,4,64,3,1280]{4,2,3,1,0:T(8,128)} %param.5) | copy-start | bytes 11796484
